TPU v7x, 32 devices: a whole 2x2x4 slice. The times are simulated.
32 devices in a mesh: grp: 2 (over x), suf: 4 (over y, core), head: 4 (over z).
Axes of the slice: x: 2, y: 2, z: 4, core: 2. Of those that a mesh axis runs over, the one named last changes fastest.
Arguments:
- prefix_x: bfloat16 [1024, 8192], P(('grp', 'suf'), 'head'), parts along dimension 0, may hold values from -6 to 6
- prefix_b: bfloat16 [1024, 1024], P(('grp', 'suf'), 'head'), parts along dimension 0, may hold values from -6 to 6
- prefix_c: bfloat16 [1024, 1024], P(('grp', 'suf'), 'head'), parts along dimension 0, may hold values from -6 to 6
- prefix_dt: float32 [128, 1024], P('head', ('grp', 'suf')), parts along dimension 1, may hold values from -3 to 3
- prefix_grad: bfloat16 [1024, 8192], P(('grp', 'suf'), 'head'), parts along dimension 0, may hold values from -0.59765625 to 0.59765625
- suffix_x: bfloat16 [8, 128, 8192], P(('grp', 'suf'), None, 'head'), parts along dimension 0, may hold values from -6 to 6
- suffix_b: bfloat16 [8, 128, 1024], P(('grp', 'suf'), None, 'head'), parts along dimension 0, may hold values from -6 to 6
- suffix_c: bfloat16 [8, 128, 1024], P(('grp', 'suf'), None, 'head'), parts along dimension 0, may hold values from -6 to 6
- suffix_dt: float32 [128, 8, 128], P('head', ('grp', 'suf')), parts along dimension 1, may hold values from -3 to 3
- suffix_grad: bfloat16 [8, 128, 8192], P(('grp', 'suf'), None, 'head'), parts along dimension 0, may hold values from -0.59765625 to 0.59765625
- lengths: int32 [8], P(('grp', 'suf')), parts along dimension 0, may hold values from 1 to 128, 384 in all
- loss_mask: int32 [8, 128], P(('grp', 'suf')), parts along dimension 0, may hold values 0 or 1
- advantage: float32 [8], P(('grp', 'suf')), parts along dimension 0, may hold values from -3 to 3
- conv_x: bfloat16 [4, 8192], P(None, 'head'), may hold values from -3 to 3
- conv_b: bfloat16 [4, 1024], P(None, 'head'), may hold values from -3 to 3
- conv_c: bfloat16 [4, 1024], P(None, 'head'), may hold values from -3 to 3
- decay_rate: float32 [128], P('head'), may hold values from 7.8125e-05 to 0.05
- dt_bias: float32 [128], P('head'), may hold values from -1 to 0.5
- skip: float32 [128], P('head'), may hold values from 0.5 to 1.5
Outputs:
- prefix_dx: bfloat16 [1024, 8192], P(('grp', 'suf'), 'head'), parts along dimension 0
- prefix_db: bfloat16 [1024, 1024], P(('grp', 'suf'), 'head'), parts along dimension 0
- prefix_dc: bfloat16 [1024, 1024], P(('grp', 'suf'), 'head'), parts along dimension 0
- prefix_ddt: float32 [128, 1024], P('head', ('grp', 'suf')), parts along dimension 1
- suffix_dx: bfloat16 [8, 128, 8192], P(('grp', 'suf'), None, 'head'), parts along dimension 0
- suffix_db: bfloat16 [8, 128, 1024], P(('grp', 'suf'), None, 'head'), parts along dimension 0
- suffix_dc: bfloat16 [8, 128, 1024], P(('grp', 'suf'), None, 'head'), parts along dimension 0
- suffix_ddt: float32 [128, 8, 128], P('head', ('grp', 'suf')), parts along dimension 1
There are 2 independent parts, one for each index of `grp`. A program takes and returns all parts, laid end to end along the dimension named above; an argument that names none is the same for every part. Nothing has to cross between parts.
Inputs may be any that keep to these rules, and one draw needn't show every extreme that they name: `lengths`: some suffix has exactly 128 tokens.
All inputs are finite; a program needn't handle non-finite values. No bound on the sum of `lengths` or of `loss_mask` on one device may be relied on, other than what follows from the above.
Results may differ from a plain program's by a relative error of at most 0.001.
Values may be sent and summed in bfloat16 or wider, within the bound.
No kernel may reach another device: no remote copies, remote signals or barrier semaphores. Data moves between devices by JAX's collectives and lax.ppermute only.
A program may use at most 128 MiB of HBM per device.

v0:
```python
import jax
import jax.numpy as jnp
from jax import lax
from jax.sharding import PartitionSpec as P

HD = 64
N = 128
KW = 4
Q = 128


EXACT_DOT = lax.Precision.HIGHEST


def from_behind(block, axis, distance):
    devices = range(lax.axis_size(axis))
    route = [(i - distance, i) for i in devices if i - distance in devices]
    return lax.ppermute(block, axis, route)


def prefix(shard, axis, combine, identity, reverse):
    length, here = (lax.axis_size(axis), lax.axis_index(axis))
    everything = jax.tree.map(lambda part: lax.all_gather(part, axis), shard)
    start = jax.tree.map(
        lambda part, zero: jnp.broadcast_to(jnp.asarray(zero, part.dtype), part.shape),
        shard,
        identity,
    )

    def lap(k, before):
        at = length - 1 - k if reverse else k
        reached = at > here if reverse else at < here
        new = combine(before, jax.tree.map(lambda part: part[at], everything))
        return jax.tree.map(lambda a, b: jnp.where(reached, a, b), new, before)

    return lax.fori_loop(0, length, lap, start)


def spread(block, axis, holder):
    block = jnp.where(lax.axis_index(axis) == holder, block, jnp.zeros_like(block))
    return lax.psum(block, axis)


def causal_conv(values, context, taps):
    padded = jnp.concatenate([context, values], axis=0)
    num_tokens = values.shape[0]
    result = padded[0:num_tokens] * taps[0].astype(jnp.float32)
    for tap_index in range(1, taps.shape[0]):
        result = result + padded[tap_index : tap_index + num_tokens] * taps[tap_index].astype(
            jnp.float32
        )
    return jax.nn.silu(result)


def run_scan(x_act, b_act, c_act, step_dt, decay_rates, skip_gain, start_state):
    tokens = x_act.shape[0]
    num_heads = x_act.shape[1]
    num_groups = b_act.shape[1]
    per_group = num_heads // num_groups
    blocks = tokens // Q
    x_blocks = x_act.reshape(blocks, Q, num_groups, per_group, HD)
    b_blocks = b_act.reshape(blocks, Q, num_groups, N)
    c_blocks = c_act.reshape(blocks, Q, num_groups, N)
    log_decay = (
        (-step_dt * decay_rates[:, None])
        .reshape(num_groups, per_group, blocks, Q)
        .transpose(2, 0, 1, 3)
    )
    dt_blocks = step_dt.reshape(num_groups, per_group, blocks, Q).transpose(2, 0, 1, 3)
    lower_tri = jnp.arange(Q)[:, None] >= jnp.arange(Q)[None, :]
    skip_shaped = skip_gain.reshape(num_groups, per_group)[:, :, None]

    def advance(current, pieces):
        x_block, b_block, c_block, log_block, dt_block = pieces
        cumulative = jnp.cumsum(log_block, axis=-1)
        log_gaps = cumulative[..., :, None] - cumulative[..., None, :]
        within = jnp.where(lower_tri, jnp.exp(jnp.where(lower_tri, log_gaps, 0.0)), 0.0)
        scores = jnp.einsum("tgn,sgn->gts", c_block, b_block, precision=EXACT_DOT)
        mixing = scores[:, None] * within * dt_block[:, :, None, :]
        inner_out = jnp.einsum("gkts,sgkp->tgkp", mixing, x_block, precision=EXACT_DOT)
        carried = jnp.einsum("tgn,gkpn->tgkp", c_block, current, precision=EXACT_DOT)
        carried = carried * jnp.exp(cumulative).transpose(2, 0, 1)[..., None]
        output = inner_out + carried + skip_shaped * x_block
        weights = jnp.exp(cumulative[..., -1:] - cumulative) * dt_block
        updated = current * jnp.exp(cumulative[..., -1])[..., None, None]
        updated = updated + jnp.einsum(
            "gks,sgkp,sgn->gkpn", weights, x_block, b_block, precision=EXACT_DOT
        )
        return (updated, output)

    last_state, outputs = lax.scan(
        jax.checkpoint(advance),
        start_state.reshape(num_groups, per_group, HD, N),
        (x_blocks, b_blocks, c_blocks, log_decay, dt_blocks),
    )
    return (outputs.reshape(tokens, num_heads * HD), last_state.reshape(num_heads, HD, N))


def block_forward(x_feat, b_feat, c_feat, dt_raw, left_x, left_b, left_c, start_state, params):
    conv_x, conv_b, conv_c, decay_rates, dt_offset, skip_gain = params
    num_heads = decay_rates.shape[0]
    num_groups = conv_b.shape[1] // N
    x_act = causal_conv(x_feat, left_x, conv_x).reshape(-1, num_heads, HD)
    b_act = causal_conv(b_feat, left_b, conv_b).reshape(-1, num_groups, N)
    c_act = causal_conv(c_feat, left_c, conv_c).reshape(-1, num_groups, N)
    step_dt = jax.nn.softplus(dt_raw + dt_offset[:, None])
    return run_scan(x_act, b_act, c_act, step_dt, decay_rates, skip_gain, start_state)


def block_grads(xa, ba, ca, step, rate, skip, S0, G, lam):
    T = xa.shape[0]
    tri = jnp.arange(T)[:, None] >= jnp.arange(T)[None, :]
    cum = jnp.cumsum(-step * rate[:, :, None], axis=-1)
    gaps = cum[..., :, None] - cum[..., None, :]
    within = jnp.where(tri, jnp.exp(jnp.where(tri, gaps, 0.0)), 0.0)
    scores = jnp.einsum("tgn,sgn->gts", ca, ba, precision=EXACT_DOT)
    score_w = scores[:, None] * within
    mixing = score_w * step[:, :, None, :]
    d_mix = jnp.einsum("tgkp,sgkp->gkts", G, xa, precision=EXACT_DOT)
    dx = jnp.einsum("gkts,tgkp->sgkp", mixing, G, precision=EXACT_DOT) + skip[None, :, :, None] * G
    d_sw = d_mix * within
    d_scores = jnp.sum(d_sw * step[:, :, None, :], axis=1)
    dc = jnp.einsum("gts,sgn->tgn", d_scores, ba, precision=EXACT_DOT)
    db = jnp.einsum("gts,tgn->sgn", d_scores, ca, precision=EXACT_DOT)
    grow = jnp.exp(cum)
    g_grow = G * grow.transpose(2, 0, 1)[..., None]
    carried = jnp.einsum("tgn,gkpn->tgkp", ca, S0, precision=EXACT_DOT)
    dc = dc + jnp.einsum("tgkp,gkpn->tgn", g_grow, S0, precision=EXACT_DOT)
    d_cum = jnp.sum(g_grow * carried, axis=-1).transpose(1, 2, 0)
    q_mat = d_mix * score_w
    d_step = jnp.sum(q_mat, axis=-2)
    p_mat = q_mat * step[:, :, None, :]
    d_cum = d_cum + jnp.sum(p_mat, axis=-1) - jnp.sum(p_mat, axis=-2)
    if lam is not None:
        to_end = jnp.exp(cum[..., -1:] - cum)
        push = to_end * step
        lam_b = jnp.einsum("gkpn,sgn->sgkp", lam, ba, precision=EXACT_DOT)
        dx = dx + push.transpose(2, 0, 1)[..., None] * lam_b
        db = db + jnp.einsum("gkpn,sgkp,gks->sgn", lam, xa, push, precision=EXACT_DOT)
        q_end = jnp.sum(xa * lam_b, axis=-1).transpose(1, 2, 0)
        d_step = d_step + to_end * q_end
        wq = push * q_end
        end_total = jnp.sum(wq, axis=-1) + jnp.exp(cum[..., -1]) * jnp.sum(lam * S0, axis=(-2, -1))
        d_cum = d_cum - wq
        d_cum = d_cum.at[..., -1].add(end_total)
    d_log = jnp.flip(jnp.cumsum(jnp.flip(d_cum, -1), axis=-1), -1)
    d_step = d_step - rate[:, :, None] * d_log
    return dx, db, dc, d_step


def shards(
    prefix_x,
    prefix_b,
    prefix_c,
    prefix_dt,
    prefix_grad,
    suffix_x,
    suffix_b,
    suffix_c,
    suffix_dt,
    suffix_grad,
    lengths,
    loss_mask,
    advantage,
    conv_x,
    conv_b,
    conv_c,
    decay_rate,
    dt_bias,
    skip,
):
    num_ways = lax.axis_size("suf")
    my_index = lax.axis_index("suf")
    num_heads = decay_rate.shape[0]
    num_groups = conv_b.shape[1] // N
    per_group = num_heads // num_groups
    margin = KW - 1
    prompt_len = prefix_x.shape[0]
    width_x = prefix_x.shape[1]
    width_b = prefix_b.shape[1]
    rate = decay_rate.reshape(num_groups, per_group)
    gain = skip.reshape(num_groups, per_group)

    def split_tokens(tokens):
        return (
            tokens[:, :width_x],
            tokens[:, width_x : width_x + width_b],
            tokens[:, width_x + width_b :],
        )

    def convs(ux, ub, uc, cx, cb, cc):
        return (
            causal_conv(ux, cx, conv_x),
            causal_conv(ub, cb, conv_b),
            causal_conv(uc, cc, conv_c),
        )

    def softplus_of(raw):
        return jax.nn.softplus(raw + dt_bias[:, None])

    prompt_step, step_pullback = jax.vjp(softplus_of, prefix_dt)
    cumulative = jnp.cumsum(-prompt_step * decay_rate[:, None], axis=1)
    total_log = cumulative[:, -1]
    tails = jnp.concatenate(
        [prefix_x[-margin:], prefix_b[-margin:], prefix_c[-margin:]], axis=1
    ).astype(jnp.float32)
    tail_size = tails.size
    every = lax.all_gather(jnp.concatenate([tails.reshape(-1), total_log]), "suf")
    every_tails = every[:, :tail_size].reshape((num_ways,) + tails.shape)
    every_log = every[:, tail_size:]
    behind = lax.dynamic_index_in_dim(every_tails, jnp.maximum(my_index - 1, 0), 0, False)
    behind = jnp.where(my_index > 0, behind, 0.0)
    left_x, left_b, left_c = split_tokens(behind)
    ctx_x, ctx_b, ctx_c = split_tokens(every_tails[num_ways - 1])

    acts, prompt_conv_pullback = jax.vjp(
        convs,
        prefix_x.astype(jnp.float32),
        prefix_b.astype(jnp.float32),
        prefix_c.astype(jnp.float32),
        left_x,
        left_b,
        left_c,
    )
    x_act = acts[0].reshape(prompt_len, num_groups, per_group, HD)
    b_act = acts[1].reshape(prompt_len, num_groups, N)
    c_act = acts[2].reshape(prompt_len, num_groups, N)
    prompt_cot = prefix_grad.astype(jnp.float32).reshape(prompt_len, num_groups, per_group, HD)
    push_weight = (jnp.exp(total_log[:, None] - cumulative) * prompt_step).reshape(
        num_groups, per_group, prompt_len
    )
    own_state = jnp.einsum("gkt,tgkp,tgn->gkpn", push_weight, x_act, b_act, precision=EXACT_DOT)
    pull_weight = jnp.exp(cumulative).reshape(num_groups, per_group, prompt_len)
    own_adjoint = jnp.einsum(
        "gkt,tgkp,tgn->gkpn", pull_weight, prompt_cot, c_act, precision=EXACT_DOT
    )
    every_pair = lax.all_gather(jnp.stack([own_state, own_adjoint]), "suf")
    every_decay = jnp.exp(every_log).reshape(num_ways, num_groups, per_group, 1, 1)
    running = jnp.zeros_like(own_state)
    start_state = running
    for block in range(num_ways):
        start_state = jnp.where(my_index == block, running, start_state)
        running = every_decay[block] * running + every_pair[block, 0]
    prompt_end = running

    positions = jnp.arange(suffix_x.shape[1])[None, :]
    weight = (
        advantage[:, None]
        * loss_mask.astype(jnp.float32)
        * (positions < lengths[:, None]).astype(jnp.float32)
    )

    def one_suffix(x_one, b_one, c_one, dt_one, grad_one, weight_one):
        suffix_len = x_one.shape[0]
        step_one, one_step_pullback = jax.vjp(softplus_of, dt_one)
        s_acts, conv_pullback = jax.vjp(convs, x_one, b_one, c_one, ctx_x, ctx_b, ctx_c)
        sx = s_acts[0].reshape(suffix_len, num_groups, per_group, HD)
        sb = s_acts[1].reshape(suffix_len, num_groups, N)
        sc = s_acts[2].reshape(suffix_len, num_groups, N)
        cot = (weight_one[:, None] * grad_one).reshape(suffix_len, num_groups, per_group, HD)
        step_g = step_one.reshape(num_groups, per_group, suffix_len)
        grow = jnp.exp(jnp.cumsum(-step_g * rate[:, :, None], axis=-1))
        adjoint = jnp.einsum("gkt,tgkp,tgn->gkpn", grow, cot, sc, precision=EXACT_DOT)
        dx, db, dc, d_step = block_grads(sx, sb, sc, step_g, rate, gain, prompt_end, cot, None)
        conv_grads = conv_pullback(
            (dx.reshape(suffix_len, -1), db.reshape(suffix_len, -1), dc.reshape(suffix_len, -1))
        )
        d_dt = one_step_pullback(d_step.reshape(num_heads, suffix_len))[0]
        return conv_grads, d_dt, adjoint

    conv_grads, suffix_ddt, adjoints = jax.vmap(one_suffix, in_axes=(0, 0, 0, 1, 0, 0), out_axes=(0, 1, 0))(
        suffix_x.astype(jnp.float32),
        suffix_b.astype(jnp.float32),
        suffix_c.astype(jnp.float32),
        suffix_dt,
        suffix_grad.astype(jnp.float32),
        weight,
    )
    summed = lax.psum(
        (jnp.sum(adjoints, axis=0), jnp.sum(conv_grads[3], axis=0), jnp.sum(conv_grads[4], axis=0)),
        "suf",
    )
    summed_c = lax.psum(jnp.sum(conv_grads[5], axis=0), "suf")
    running = summed[0]
    end_grad = running
    for block in reversed(range(num_ways)):
        end_grad = jnp.where(my_index == block, running, end_grad)
        running = every_pair[block, 1] + every_decay[block] * running

    step_g = prompt_step.reshape(num_groups, per_group, prompt_len)
    dx, db, dc, d_step = block_grads(
        x_act, b_act, c_act, step_g, rate, gain, start_state, prompt_cot, end_grad
    )
    prompt_grads = prompt_conv_pullback(
        (dx.reshape(prompt_len, -1), db.reshape(prompt_len, -1), dc.reshape(prompt_len, -1))
    )
    prefix_ddt = step_pullback(d_step.reshape(num_heads, prompt_len))[0]
    left_grads = jnp.concatenate([prompt_grads[3], prompt_grads[4], prompt_grads[5]], axis=1)
    from_right = from_behind(left_grads, "suf", -1)
    last_device = my_index == num_ways - 1
    from_suffix = jnp.concatenate([summed[1], summed[2], summed_c], axis=1)
    tail_add = split_tokens(from_right + jnp.where(last_device, from_suffix, 0.0))

    def finish(grad_full, extra):
        return grad_full.at[-margin:].add(extra).astype(jnp.bfloat16)

    return (
        finish(prompt_grads[0], tail_add[0]),
        finish(prompt_grads[1], tail_add[1]),
        finish(prompt_grads[2], tail_add[2]),
        prefix_ddt,
        conv_grads[0].astype(jnp.bfloat16),
        conv_grads[1].astype(jnp.bfloat16),
        conv_grads[2].astype(jnp.bfloat16),
        suffix_ddt,
    )


def solution(mesh):
    return jax.shard_map(
        shards,
        mesh=mesh,
        in_specs=(
            P(("grp", "suf"), "head"),
            P(("grp", "suf"), "head"),
            P(("grp", "suf"), "head"),
            P("head", ("grp", "suf")),
            P(("grp", "suf"), "head"),
            P(("grp", "suf"), None, "head"),
            P(("grp", "suf"), None, "head"),
            P(("grp", "suf"), None, "head"),
            P("head", ("grp", "suf"), None),
            P(("grp", "suf"), None, "head"),
            P(("grp", "suf")),
            P(("grp", "suf"), None),
            P(("grp", "suf")),
            P(None, "head"),
            P(None, "head"),
            P(None, "head"),
            P("head"),
            P("head"),
            P("head"),
        ),
        out_specs=(
            P(("grp", "suf"), "head"),
            P(("grp", "suf"), "head"),
            P(("grp", "suf"), "head"),
            P("head", ("grp", "suf")),
            P(("grp", "suf"), None, "head"),
            P(("grp", "suf"), None, "head"),
            P(("grp", "suf"), None, "head"),
            P("head", ("grp", "suf"), None),
        ),
        check_vma=False,
    )
```

profile of v0, /device:TPU:1, one launch (start us, length us, event | category | flops | bytes accessed | tf_op | source)
XLA Modules:
  0.0 262.6 jit_solution(63715825391042475)
XLA Ops:
  7.3 1.5 compare_select_fusion.7
  11.4 1.2 dynamic-slice.32
  15.8 1.4 exponential_multiply_fusion.1
  17.2 1.4 slice_convert_fusion.14
  20.1 1.3 copy.262
  22.7 1.5 slice_convert_fusion.6
  26.4 1.3 copy.253
  27.8 19.0 %all-reduce.31.cloned.1.call-done = f32[30848]{0:T(1024)} async-done(((f32[30848]{0:T(1024)}), f32[30848]{0:T(1024)}) %all-reduce.31.cloned.1.call-update) | async-done | bytes 123408
  48.1 1.5 fusion.129
  49.7 2.8 %fusion.69 = f32[2,16,64,128]{3,2,1,0:T(8,128)} fusion(f32[128,2,16,64]{0,3,2,1:T(8,128)S(1)} %bitcast.285, f32[128,2,16]{0,2,1:T(8,128)} %exponential_bitcast_fusion.2, f32[128,2,128,1]{2,1,0,3:T(2,128)S(1)} %bitcast.297), kind=kOutput, calls=%fused_computation.109 | convolution fusion | flops 402915328 | bytes 2244608 | tf_op jit(solution)/shard_map/vmap(gkt,tgkp,tgn->gkpn)/dot_general | solution.py:263
  52.6 2.0 fusion.72
  55.7 1.5 copy.259
  57.2 1.1 convolution_bitcast_fusion.3
  58.3 1.0 convolution_bitcast_fusion.4
  59.4 1.5 pad_maximum_fusion
  62.2 1.3 copy.276
  63.5 1.1 convert_element_type.150
  69.0 1.3 exponential_bitcast_fusion
  70.4 1.4 compare_select_fusion.5
  73.2 1.4 slice_bitcast_fusion.8
  74.6 2.1 copy.277
  78.0 1.3 mul.887
  79.3 1.3 mul.889
  80.6 1.3 mul.891
  82.0 1.3 mul.934
  84.0 3.3 %fusion.22 = f32[1,128,2,16,64]{1,4,3,2,0:T(8,128)S(1)} fusion(f32[128,2,16,64]{0,3,2,1:T(8,128)S(1)} %bitcast.286, f32[1,128,2,16,64]{1,4,3,2,0:T(8,128)S(1)} %bitcast.287, f32[2,16,128]{2,1,0:T(8,128)} %compare_select_fusion.5, f32[2,16,128]{2,1,0:T(8,128)} %bitcast.331, f32[2,128,128]{2,1,0:T(8,128)S(1)} %fusion.170, ...), kind=kOutput, calls=%fused_computation.41 | convolution fusion | flops 405798912 | bytes 3326080 | tf_op jit(solution)/shard_map/vmap(gkts,tgkp->sgkp)/dot_general | solution.py:120
  87.4 1.1 fusion.169
  88.9 3.9 %broadcast_multiply_fusion = (f32[1,128,2048]{1,2,0:T(8,128)}, f32[1,128,2048]{1,2,0:T(8,128)}, f32[1,128,2048]{1,2,0:T(8,128)S(1)}) fusion(f32[2048]{0:T(1024)S(1)} %bitcast.335, f32[1,128,2,16,64]{1,4,3,2,0:T(8,128)S(1)} %fusion.22, f32[1,128,2048]{1,2,0:T(8,128)S(1)} %copy-done.11, f32[2048]{0:T(1024)S(1)} %bitcast.323, f32[1,3,2048]{1,2,0:T(8,128)S(1)} %copy-done.12, ...), kind=kLoop, calls=%fused_computation.124 | loop fusion | flops 5242880 | bytes 5300224 | tf_op jit(solution)/shard_map/vmap(transpose(jvp()))/mul | solution.py:49
  93.6 7.3 %multiply_reduce_fusion.2 = (f32[2,16,128]{2,1,0:T(8,128)}, f32[2,16,128]{2,1,0:T(8,128)}, f32[2,16,128]{2,1,0:T(8,128)}, f32[2,128,128]{2,1,0:T(8,128)S(1)}, f3...) fusion(f32[2,16,128]{2,1,0:T(8,128)S(1)} %copy-done.78, ...), kind=kOutput, calls=%fused_computation.21 | convolution fusion | flops 415145984 | bytes 4898816 | tf_op jit(solution)/shard_map/vmap(tgkp,sgkp->gkts)/dot_general | solution.py:119
  102.7 2.3 broadcast_multiply_fusion.1
  105.0 1.7 pad_add_fusion
  106.7 1.4 copy-done.9
  109.3 1.2 broadcast_multiply_fusion.8
  111.9 2.0 convolution_bitcast_fusion.5
  114.5 1.0 slice_bitcast_fusion.1
  115.6 35.6 %all-gather.4.cloned.1.call-done = f32[8,2,16,64,128]{4,3,2,1,0:T(8,128)} async-done(((f32[2,2,16,64,128]{4,3,2,1,0:T(8,128)}), f32[8,2,16,64,128]{4,3,2,1,0:T(8,128)}) %all-gather.4.cloned.1.call-update) | async-done | bytes 8388624 | tf_op jit(solution)/shard_map/all_gather | solution.py:237
  151.1 6.3 %multiply_reduce_fusion.5 = (f32[2,16]{1,0:T(2,128)}, f32[2,16,64,128]{3,2,1,0:T(8,128)S(1)}, f32[2,16,64,128]{3,2,1,0:T(8,128)}, f32[2,16,64,128]{3,2,1,0:T(8,128)}) fusion(pred[]{:T(512)S(6)} %eq.40, pred[]{:T(512)S(6)} %eq.41, f32[4,2,2,16,64,128]{5,4,3,2,1,0:T(8,128)} %bitcast.296, f32[2,16]{1,0:T(2,128)} %mul.934, f32[2,16]{1,0:T(2,128)} %mul.887, ...), kind=kLoop, calls=%fused_computation.98 | loop fusion | flops 5504992 | bytes 11534980 | tf_op jit(solution)/shard_map/reduce_sum | solution.py:143
  157.4 1.7 fusion.30
  159.1 1.9 fusion.31
  164.5 2.6 multiply_reduce_fusion.6
  168.0 2.3 fusion.140
  171.0 3.9 %fusion.25 = f32[128,2,16,64]{0,3,2,1:T(8,128)} fusion(bf16[128,2,16,64]{0,3,2,1:T(8,128)(2,1)S(1)} %bitcast.295, f32[128,2,16,64]{0,3,2,1:T(8,128)} %get-tuple-element.196, f32[2,16,128]{2,1,0:T(8,128)} %bitcast.339, f32[2,16,128]{2,1,0:T(8,128)} %copy-done.48, f32[2,128,128]{2,1,0:T(8,128)} %copy-done.55, pred[128,128]{1,0:T(8,128)(4,1)} %iota_compare_fusion, ...), kind=kOutput, calls=%fused_computation.42 | convolution fusion | flops 406585344 | bytes 2818176 | tf_op jit(solution)/shard_map/gkts,tgkp->sgkp/dot_general | solution.py:120
  174.9 2.5 copy.265
  177.4 2.0 broadcast_multiply_fusion.4
  181.5 1.2 pad_add_fusion.1
  182.7 1.1 fusion.29
  185.3 1.5 exponential_multiply_fusion
  187.7 1.6 bitcast_add_fusion
  191.8 1.1 fusion.141
  195.3 1.3 add.343
  197.5 1.4 multiply_subtract_fusion
  199.9 1.4 fusion.146
  201.3 3.0 %fusion.33 = f32[1,128,2,128]{1,3,2,0:T(8,128)S(1)} fusion(f32[1,128,2,128]{1,3,2,0:T(8,128)} %convolution_bitcast_fusion.5, f32[2,16,64,128]{3,2,1,0:T(8,128)} %get-tuple-element.151, f32[128,2,16,64]{0,3,2,1:T(8,128)S(1)} %bitcast.290, f32[128,2,16]{0,2,1:T(8,128)S(1)} %copy-done.47), kind=kOutput, calls=%fused_computation.53 | convolution fusion | flops 402948096 | bytes 2375680 | tf_op jit(solution)/shard_map/vmap(tgkp,gkpn->tgn)/dot_general | solution.py:128
  205.1 1.1 broadcast_multiply_fusion.12
  207.7 2.5 convolution_bitcast_fusion.8
  211.7 2.3 collective-permute-start
  214.6 1.5 split.67
  216.9 27.8 %all-reduce.25 = (f32[3,256]{1,0:T(4,128)S(1)}, f32[3,256]{1,0:T(4,128)S(1)}, f32[3,2048]{0,1:T(8,128)}) all-reduce(f32[3,256]{1,0:T(4,128)} %slice_bitcast_fusion.9, f32[3,256]{1,0:T(4,128)} %slice_bitcast_fusion.10, f32[3,2048]{0,1:T(8,128)} %slice_bitcast_fusion.1), channel_id=1, replica_groups=mesh['grp'=2,'suf'=4,'head'=4] {'suf'}, use_global_device_ids=true, to_apply=%region_8.9 | all-reduce | flops 7680 | bytes 61440 | tf_op jit(solution)/shard_map/psum | solution.py:283
  244.6 2.2 copy.284
  246.8 1.6 split.55
  248.4 2.0 split.51
  252.0 1.3 scatter-add.16
  253.3 1.3 scatter-add.15
  254.6 1.4 scatter-add.14
  (284 shorter events, 48.8 us)
Async XLA Ops:
  7.2 19.1 %copy-start.32 = (bf16[128,2048]{1,0:T(8,128)(2,1)S(1)}, bf16[128,2048]{1,0:T(8,128)(2,1)}, u32[]{:S(2)}) copy-start(bf16[128,2048]{1,0:T(8,128)(2,1)} %param.27) | copy-start | bytes 1572868
  7.2 19.0 %copy-start.57 = (bf16[128,256]{1,0:T(8,128)(2,1)S(1)}, bf16[128,256]{1,0:T(8,128)(2,1)}, u32[]{:S(2)}) copy-start(bf16[128,256]{1,0:T(8,128)(2,1)} %param.28) | copy-start | bytes 196612
  7.2 19.0 %copy-start.56 = (bf16[128,256]{1,0:T(8,128)(2,1)S(1)}, bf16[128,256]{1,0:T(8,128)(2,1)}, u32[]{:S(2)}) copy-start(bf16[128,256]{1,0:T(8,128)(2,1)} %param.29) | copy-start | bytes 196612
  7.2 18.4 %copy-start.82 = (bf16[4,256]{1,0:T(4,128)(2,1)S(1)}, bf16[4,256]{1,0:T(4,128)(2,1)}, u32[]{:S(2)}) copy-start(bf16[4,256]{1,0:T(4,128)(2,1)} %param.41) | copy-start | bytes 6148
  7.2 39.5 %all-reduce.31.cloned.1.call-start = ((), (), s32[]{:S(2)}) async-start(), calls=%async_computation.2 | async-start | bytes 253952
  14.2 101.3 %all-reduce.29.cloned.1.call-start = ((), (), s32[]{:S(2)}) async-start(), calls=%async_computation | async-start | bytes 2097152 | tf_op jit(solution)/shard_map/psum | solution.py:279
  15.0 4.4 %copy-start.76 = (f32[2,16]{1,0:T(2,128)}, f32[2,16]{1,0:T(2,128)S(1)}, u32[]{:S(2)}) copy-start(f32[2,16]{1,0:T(2,128)S(1)} %mul.858) | copy-start | bytes 388
  15.8 3.7 %copy-start.83 = (f32[2,16]{1,0:T(2,128)}, f32[2,16]{1,0:T(2,128)S(1)}, u32[]{:S(2)}) copy-start(f32[2,16]{1,0:T(2,128)S(1)} %add.307) | copy-start | bytes 388
  20.1 6.3 %copy-start.50 = (f32[1,2,16,128]{3,2,1,0:T(8,128)}, f32[1,2,16,128]{3,2,1,0:T(8,128)S(1)}, u32[]{:S(2)}) copy-start(f32[1,2,16,128]{3,2,1,0:T(8,128)S(1)} %reduce_window_sum.50) | copy-start | bytes 49156
  20.1 6.3 %copy-start.60 = (bf16[1,128,256]{2,1,0:T(8,128)(2,1)S(1)}, bf16[1,128,256]{2,1,0:T(8,128)(2,1)}, u32[]{:S(2)}) copy-start(bf16[1,128,256]{2,1,0:T(8,128)(2,1)} %param.34) | copy-start | bytes 196612
  21.4 5.0 %copy-start.61 = (bf16[1,128,256]{2,1,0:T(8,128)(2,1)S(1)}, bf16[1,128,256]{2,1,0:T(8,128)(2,1)}, u32[]{:S(2)}) copy-start(bf16[1,128,256]{2,1,0:T(8,128)(2,1)} %param.33) | copy-start | bytes 196612
  24.2 28.4 %copy-start.41 = (f32[1,2048]{1,0:T(1,128)}, f32[1,2048]{1,0:T(1,128)S(1)}, u32[]{:S(2)}) copy-start(f32[1,2048]{1,0:T(1,128)S(1)} %get-tuple-element.186) | copy-start | bytes 24580
  47.8 4.7 %copy-start.31 = (f32[4,7712]{1,0:T(4,128)}, f32[4,7712]{1,0:T(4,128)S(1)}, u32[]{:S(2)}) copy-start(f32[4,7712]{1,0:T(4,128)S(1)} %reshape.596) | copy-start | bytes 370180
  48.0 4.5 %copy-start.45 = (f32[3,2560]{1,0:T(4,128)}, f32[3,2560]{1,0:T(4,128)S(1)}, u32[]{:S(2)}) copy-start(f32[3,2560]{1,0:T(4,128)S(1)} %squeeze.24) | copy-start | bytes 92164
  48.0 4.6 %copy-start.52 = (f32[1,2048]{1,0:T(1,128)S(1)}, f32[1,2048]{1,0:T(1,128)}, u32[]{:S(2)}) copy-start(f32[1,2048]{1,0:T(1,128)} %get-tuple-element.185) | copy-start | bytes 24580
  52.5 2.2 copy-start.67
  52.5 2.2 copy-start.69
  52.5 2.2 copy-start.71
  52.5 2.2 copy-start.72
  52.5 2.2 copy-start.73
  52.5 2.2 copy-start.74
  52.5 98.6 %all-gather.4.cloned.1.call-start = ((), (), s32[]{:S(2)}) async-start(), calls=%async_computation.1 | async-start | bytes 10485760 | tf_op jit(solution)/shard_map/all_gather | solution.py:237
  54.6 2.6 %copy-start.59 = (f32[32,128]{1,0:T(8,128)S(1)}, f32[32,128]{1,0:T(8,128)}, u32[]{:S(2)}) copy-start(f32[32,128]{1,0:T(8,128)} %get-tuple-element.182) | copy-start | bytes 49156
  55.6 2.7 %copy-start.58 = (f32[32,128]{1,0:T(8,128)S(1)}, f32[32,128]{1,0:T(8,128)}, u32[]{:S(2)}) copy-start(f32[32,128]{1,0:T(8,128)} %get-tuple-element.181) | copy-start | bytes 49156
  65.4 6.7 %copy-start.24 = (f32[2,16,128]{1,0,2:T(2,128)}, f32[2,16,128]{1,0,2:T(2,128)S(1)}, u32[]{:S(2)}) copy-start(f32[2,16,128]{1,0,2:T(2,128)S(1)} %copy.251) | copy-start | bytes 49156
  66.9 3.5 %copy-start.48 = (f32[2,16,128]{2,1,0:T(8,128)}, f32[2,16,128]{2,1,0:T(8,128)S(1)}, u32[]{:S(2)}) copy-start(f32[2,16,128]{2,1,0:T(8,128)S(1)} %reduce_window_sum.49) | copy-start | bytes 49156
  67.0 3.3 %copy-start.81 = (f32[2,16,1]{1,0,2:T(2,128)}, f32[2,16,1]{1,0,2:T(2,128)S(1)}, u32[]{:S(2)}) copy-start(f32[2,16,1]{1,0,2:T(2,128)S(1)} %copy.324) | copy-start | bytes 388
  72.0 15.4 %copy-start.26 = (f32[128,2,128]{0,2,1:T(8,128)}, f32[128,2,128]{0,2,1:T(8,128)S(1)}, u32[]{:S(2)}) copy-start(f32[128,2,128]{0,2,1:T(8,128)S(1)} %copy.267) | copy-start | bytes 393220
  72.1 15.3 %copy-start.28 = (f32[128,2,128]{0,2,1:T(8,128)}, f32[128,2,128]{0,2,1:T(8,128)S(1)}, u32[]{:S(2)}) copy-start(f32[128,2,128]{0,2,1:T(8,128)S(1)} %copy.271) | copy-start | bytes 393220
  73.2 14.2 %copy-start.23 = (f32[1,128,256]{1,2,0:T(8,128)}, f32[1,128,256]{1,2,0:T(8,128)S(1)}, u32[]{:S(2)}) copy-start(f32[1,128,256]{1,2,0:T(8,128)S(1)} %copy.325) | copy-start | bytes 393220
  84.0 9.1 %copy-start.55 = (f32[2,128,128]{2,1,0:T(8,128)}, f32[2,128,128]{2,1,0:T(8,128)S(1)}, u32[]{:S(2)}) copy-start(f32[2,128,128]{2,1,0:T(8,128)S(1)} %fusion.168) | copy-start | bytes 393220
  93.6 9.1 %copy-start.43 = (f32[1,2048]{1,0:T(1,128)S(1)}, f32[1,2048]{1,0:T(1,128)}, u32[]{:S(2)}) copy-start(f32[1,2048]{1,0:T(1,128)} %copy-done.41) | copy-start | bytes 24580
  100.9 4.1 %copy-start.33 = (f32[2,128,128]{2,1,0:T(8,128)}, f32[2,128,128]{2,1,0:T(8,128)S(1)}, u32[]{:S(2)}) copy-start(f32[2,128,128]{2,1,0:T(8,128)S(1)} %get-tuple-element.110) | copy-start | bytes 393220
  102.7 2.4 copy-start.13
  109.3 5.2 %copy-start.10 = (f32[1,131,2048]{1,2,0:T(8,128)S(1)}, f32[1,131,2048]{1,2,0:T(8,128)}, u32[]{:S(2)}) copy-start(f32[1,131,2048]{1,2,0:T(8,128)} %copy-done.9) | copy-start | bytes 3219460
  151.1 6.3 %copy-start.46 = (f32[128,2,16]{0,2,1:T(8,128)S(1)}, f32[128,2,16]{0,2,1:T(8,128)}, u32[]{:S(2)}) copy-start(f32[128,2,16]{0,2,1:T(8,128)} %get-tuple-element.179) | copy-start | bytes 49156
  157.4 3.6 %copy-start.29 = (f32[128,2,128]{0,2,1:T(8,128)S(1)}, f32[128,2,128]{0,2,1:T(8,128)}, u32[]{:S(2)}) copy-start(f32[128,2,128]{0,2,1:T(8,128)} %copy-done.28) | copy-start | bytes 393220
  157.4 3.6 %copy-start.36 = (f32[2,128,128]{2,1,0:T(8,128)S(1)}, f32[2,128,128]{2,1,0:T(8,128)}, u32[]{:S(2)}) copy-start(f32[2,128,128]{2,1,0:T(8,128)} %get-tuple-element.112) | copy-start | bytes 393220
  157.4 4.1 %copy-start.35 = (f32[128,256]{1,0:T(8,128)S(1)}, f32[128,256]{1,0:T(8,128)}, u32[]{:S(2)}) copy-start(f32[128,256]{1,0:T(8,128)} %get-tuple-element.198) | copy-start | bytes 393220
  161.6 2.9 %copy-start.6 = (f32[2,16,64,128]{3,2,1,0:T(8,128)S(1)}, f32[2,16,64,128]{3,2,1,0:T(8,128)}, u32[]{:S(2)}) copy-start(f32[2,16,64,128]{3,2,1,0:T(8,128)} %get-tuple-element.127) | copy-start | bytes 3145732
  163.1 4.0 %copy-start.14 = (f32[128,256]{1,0:T(8,128)}, f32[128,256]{1,0:T(8,128)S(1)}, u32[]{:S(2)}) copy-start(f32[128,256]{1,0:T(8,128)S(1)} %get-tuple-element.168) | copy-start | bytes 393220
  163.1 4.0 %copy-start.16 = (f32[128,256]{1,0:T(8,128)}, f32[128,256]{1,0:T(8,128)S(1)}, u32[]{:S(2)}) copy-start(f32[128,256]{1,0:T(8,128)S(1)} %get-tuple-element.169) | copy-start | bytes 393220
  163.1 4.0 %copy-start.18 = (f32[128,256]{1,0:T(8,128)}, f32[128,256]{1,0:T(8,128)S(1)}, u32[]{:S(2)}) copy-start(f32[128,256]{1,0:T(8,128)S(1)} %get-tuple-element.170) | copy-start | bytes 393220
  163.9 4.0 %copy-start.25 = (f32[2,16,128]{1,0,2:T(2,128)S(1)}, f32[2,16,128]{1,0,2:T(2,128)}, u32[]{:S(2)}) copy-start(f32[2,16,128]{1,0,2:T(2,128)} %copy-done.24) | copy-start | bytes 49156
  167.9 6.9 %copy-start.30 = (f32[128,2,16]{2,1,0:T(2,128)}, f32[128,2,16]{2,1,0:T(2,128)S(1)}, u32[]{:S(2)}) copy-start(f32[128,2,16]{2,1,0:T(2,128)S(1)} %copy.285) | copy-start | bytes 49156
  204.4 3.4 %copy-start.7 = (f32[2,16,64,128]{3,2,1,0:T(8,128)S(1)}, f32[2,16,64,128]{3,2,1,0:T(8,128)}, u32[]{:S(2)}) copy-start(f32[2,16,64,128]{3,2,1,0:T(8,128)} %get-tuple-element.127) | copy-start | bytes 3145732
  204.4 5.9 %copy-start.27 = (f32[128,2,128]{0,2,1:T(8,128)S(1)}, f32[128,2,128]{0,2,1:T(8,128)}, u32[]{:S(2)}) copy-start(f32[128,2,128]{0,2,1:T(8,128)} %copy-done.26) | copy-start | bytes 393220
  205.1 5.1 %copy-start.37 = (f32[2,128,128]{2,1,0:T(8,128)S(1)}, f32[2,128,128]{2,1,0:T(8,128)}, u32[]{:S(2)}) copy-start(f32[2,128,128]{2,1,0:T(8,128)} %get-tuple-element.112) | copy-start | bytes 393220
  206.2 4.5 %copy-start.34 = (f32[128,256]{1,0:T(8,128)S(1)}, f32[128,256]{1,0:T(8,128)}, u32[]{:S(2)}) copy-start(f32[128,256]{1,0:T(8,128)} %get-tuple-element.146) | copy-start | bytes 393220
  206.2 4.5 %copy-start.70 = (f32[1,256]{1,0:T(1,128)S(1)}, f32[1,256]{1,0:T(1,128)}, u32[]{:S(2)}) copy-start(f32[1,256]{1,0:T(1,128)} %get-tuple-element.189) | copy-start | bytes 3076
  207.0 3.8 %copy-start.64 = (f32[1,256]{1,0:T(1,128)S(1)}, f32[1,256]{1,0:T(1,128)}, u32[]{:S(2)}) copy-start(f32[1,256]{1,0:T(1,128)} %get-tuple-element.187) | copy-start | bytes 3076
  207.0 3.8 %copy-start.66 = (f32[1,256]{1,0:T(1,128)S(1)}, f32[1,256]{1,0:T(1,128)}, u32[]{:S(2)}) copy-start(f32[1,256]{1,0:T(1,128)} %get-tuple-element.188) | copy-start | bytes 3076
  207.0 3.8 %copy-start.68 = (f32[1,256]{1,0:T(1,128)S(1)}, f32[1,256]{1,0:T(1,128)}, u32[]{:S(2)}) copy-start(f32[1,256]{1,0:T(1,128)} %get-tuple-element.190) | copy-start | bytes 3076
  210.3 5.9 %copy-start.40 = (bf16[131,256]{1,0:T(8,128)(2,1)S(1)}, bf16[131,256]{1,0:T(8,128)(2,1)}, u32[]{:S(2)}) copy-start(bf16[131,256]{1,0:T(8,128)(2,1)} %pad_add_fusion.4) | copy-start | bytes 201220
  210.8 5.4 %copy-start.19 = (f32[128,256]{1,0:T(8,128)}, f32[128,256]{1,0:T(8,128)S(1)}, u32[]{:S(2)}) copy-start(f32[128,256]{1,0:T(8,128)S(1)} %get-tuple-element.135) | copy-start | bytes 393220
  210.9 5.3 %copy-start.20 = (f32[128,256]{1,0:T(8,128)}, f32[128,256]{1,0:T(8,128)S(1)}, u32[]{:S(2)}) copy-start(f32[128,256]{1,0:T(8,128)S(1)} %get-tuple-element.165) | copy-start | bytes 393220
  210.9 5.3 %copy-start.21 = (f32[128,256]{1,0:T(8,128)}, f32[128,256]{1,0:T(8,128)S(1)}, u32[]{:S(2)}) copy-start(f32[128,256]{1,0:T(8,128)S(1)} %get-tuple-element.166) | copy-start | bytes 393220
  210.9 5.3 %copy-start.22 = (f32[128,256]{1,0:T(8,128)}, f32[128,256]{1,0:T(8,128)S(1)}, u32[]{:S(2)}) copy-start(f32[128,256]{1,0:T(8,128)S(1)} %get-tuple-element.167) | copy-start | bytes 393220
  211.7 39.5 %copy-start.15 = (f32[128,256]{1,0:T(8,128)S(1)}, f32[128,256]{1,0:T(8,128)}, u32[]{:S(2)}) copy-start(f32[128,256]{1,0:T(8,128)} %copy-done.14) | copy-start | bytes 393220
  211.7 39.6 %copy-start.17 = (f32[128,256]{1,0:T(8,128)S(1)}, f32[128,256]{1,0:T(8,128)}, u32[]{:S(2)}) copy-start(f32[128,256]{1,0:T(8,128)} %copy-done.16) | copy-start | bytes 393220
  211.7 38.7 %collective-permute-start = (f32[3,2560]{1,0:T(4,128)}, f32[3,2560]{1,0:T(4,128)}, u32[]{:S(2)}, u32[]{:S(2)}) collective-permute-start(f32[3,2560]{1,0:T(4,128)} %pad_maximum_fusion.7), channel_id=1, source_target_pairs={{4,0},{8,4},{12,8},{5,1},{9,5},{13,9},{6,2},{10,6},{14,10},{7,3},{... | collective-permute-start | bytes 92168 | tf_op jit(solution)/shard_map/ppermute | solution.py:18
  216.9 35.1 %copy-start.1 = (f32[128,2048]{1,0:T(8,128)S(1)}, f32[128,2048]{1,0:T(8,128)}, u32[]{:S(2)}) copy-start(f32[128,2048]{1,0:T(8,128)} %copy-done) | copy-start | bytes 3145732
  216.9 35.1 %copy-start.3 = (f32[128,2048]{1,0:T(8,128)S(1)}, f32[128,2048]{1,0:T(8,128)}, u32[]{:S(2)}) copy-start(f32[128,2048]{1,0:T(8,128)} %copy-done.2) | copy-start | bytes 3145732
  246.8 5.2 %copy-start.5 = (f32[128,2048]{1,0:T(8,128)S(1)}, f32[128,2048]{1,0:T(8,128)}, u32[]{:S(2)}) copy-start(f32[128,2048]{1,0:T(8,128)} %copy-done.4) | copy-start | bytes 3145732
  (25 other events, 29.4 us)
Sparse Core Ops, SparseCore 0:
  14.4 32.3 all-reduce.30
  52.6 37.3 all-reduce.28
  91.6 59.4 all-gather.3
where the time goes:
time: 266 us; the launch traced here: 263 us
  other arithmetic  62.7 us (24%)
  local copies, waits for them, and re-layouts  61.1 us (23%)
  waiting for transfers between devices  54.6 us (21%)
  matrix products  37 us (14%)
  blocking collectives  27.8 us (10%)
  between operations  17 us (6%)
    all_gather x1, waiting for transfers between devices, shards(): every_pair = lax.all_gather(jnp.stack([own_state, own_adjoint]), 'suf')  35.6 us
    psum x1, blocking collectives, shards(): summed_c = lax.psum(jnp.sum(conv_grads[5], axis=0), 'suf')  27.8 us
    unnamed x4, waiting for transfers between devices  19 us
    mul x12, other arithmetic, causal_conv(): padded[tap_index:tap_index + num_tokens]  13.9 us
    unnamed x178, local copies, waits for them, and re-layouts  11.8 us
    dot_general x2, matrix products, block_grads(): d_mix = jnp.einsum('tgkp,sgkp->gkts', G, xa, precision=EXACT_DOT)  8.37 us
    dot_general x2, matrix products, block_grads(): jnp.einsum('gkts,tgkp->sgkp', mixing, G, precision=EXACT_DOT)  7.15 us
    split x6, local copies, waits for them, and re-layouts, causal_conv(): padded = jnp.concatenate([context, values], axis=0)  6.64 us
  transfers between devices with their start and end apart: 4, of which 2 were waited for; matrix products, arithmetic and copies ran while one was open for 31% of the time, Pallas kernels for 0%

commit v1 on v0

--- a/solution.py
+++ b/solution.py
@@ -205,7 +205,14 @@
         [prefix_x[-margin:], prefix_b[-margin:], prefix_c[-margin:]], axis=1
     ).astype(jnp.float32)
     tail_size = tails.size
-    every = lax.all_gather(jnp.concatenate([tails.reshape(-1), total_log]), "suf")
+    own_pack = jnp.concatenate([tails.reshape(-1), total_log])
+    received = [own_pack] + [
+        lax.ppermute(own_pack, "suf", [(j, (j + shift) % num_ways) for j in range(num_ways)])
+        for shift in range(1, num_ways)
+    ]
+    every = jnp.take(
+        jnp.stack(received), (my_index - jnp.arange(num_ways)) % num_ways, axis=0
+    )
     every_tails = every[:, :tail_size].reshape((num_ways,) + tails.shape)
     every_log = every[:, tail_size:]
     behind = lax.dynamic_index_in_dim(every_tails, jnp.maximum(my_index - 1, 0), 0, False)
@@ -276,12 +283,15 @@
         suffix_grad.astype(jnp.float32),
         weight,
     )
-    summed = lax.psum(
-        (jnp.sum(adjoints, axis=0), jnp.sum(conv_grads[3], axis=0), jnp.sum(conv_grads[4], axis=0)),
-        "suf",
-    )
-    summed_c = lax.psum(jnp.sum(conv_grads[5], axis=0), "suf")
-    running = summed[0]
+    suffix_total = lax.psum(jnp.sum(adjoints, axis=0), "suf")
+    ctx_grads = jnp.concatenate(
+        [jnp.sum(conv_grads[3], axis=0), jnp.sum(conv_grads[4], axis=0), jnp.sum(conv_grads[5], axis=0)],
+        axis=1,
+    )
+    from_suffix = ctx_grads
+    for sender in range(num_ways - 1):
+        from_suffix = from_suffix + lax.ppermute(ctx_grads, "suf", [(sender, num_ways - 1)])
+    running = suffix_total
     end_grad = running
     for block in reversed(range(num_ways)):
         end_grad = jnp.where(my_index == block, running, end_grad)
@@ -298,7 +308,6 @@
     left_grads = jnp.concatenate([prompt_grads[3], prompt_grads[4], prompt_grads[5]], axis=1)
     from_right = from_behind(left_grads, "suf", -1)
     last_device = my_index == num_ways - 1
-    from_suffix = jnp.concatenate([summed[1], summed[2], summed_c], axis=1)
     tail_add = split_tokens(from_right + jnp.where(last_device, from_suffix, 0.0))
 
     def finish(grad_full, extra):

time: 266 us -> 235 us (0.88)
  blocking collectives: 27.8 us -> 0 us
  waiting for transfers between devices: 54.6 us -> 32 us
  starting transfers between devices: 2.41 us -> 10.7 us
  local copies, waits for them, and re-layouts: 61.1 us -> 65.7 us
  other arithmetic: 62.7 us -> 67.1 us
    psum x1 -> x0, blocking collectives: 27.8 us -> none  [shards(): summed_c = lax.psum(jnp.sum(conv_grads[5], axis=0), 'suf')]
    unnamed x4 -> x2, waiting for transfers between devices: 19 us -> 0.03 us
    ppermute x0 -> x6, starting transfers between devices: none -> 8.27 us  [the longest x3 5.12 us: shards(): lax.ppermute(ctx_grads, 'suf', [(sender, num_ways - 1)])]
    rev x4, local copies, waits for them, and re-layouts: 0.26 us -> 5.96 us  [block_grads(): d_log = jnp.flip(jnp.cumsum(jnp.flip(d_cum, -1), axis=-1), -1)]
    all_gather x1, waiting for transfers between devices: 35.6 us -> 31.9 us  [shards(): every_pair = lax.all_gather(jnp.stack([own_state, own_adjoint]), 'suf')]
    broadcast_in_dim x3 -> x1, local copies, waits for them, and re-layouts: 3.55 us -> 0.01 us  [causal_conv(): padded = jnp.concatenate([context, values], axis=0)]
    unnamed x178 -> x183, local copies, waits for them, and re-layouts: 11.8 us -> 10.8 us
  transfers between devices with their start and end apart: 4 -> 9, of which waited for: 2 -> 1; matrix products, arithmetic and copies ran while one was open for 31% -> 60% of each run, Pallas kernels for 0% -> 0%
where the time goes in v1:
time: 235 us; the launch traced here: 232 us
  other arithmetic  67.1 us (29%)
  local copies, waits for them, and re-layouts  65.7 us (28%)
  matrix products  39.4 us (17%)
  waiting for transfers between devices  32 us (14%)
  between operations  16.8 us (7%)
  starting transfers between devices  10.7 us (5%)
    all_gather x1, waiting for transfers between devices, shards(): every_pair = lax.all_gather(jnp.stack([own_state, own_adjoint]), 'suf')  31.9 us
    mul x12, other arithmetic, causal_conv(): padded[tap_index:tap_index + num_tokens]  14 us
    unnamed x183, local copies, waits for them, and re-layouts  10.8 us
    dot_general x2, matrix products, block_grads(): d_mix = jnp.einsum('tgkp,sgkp->gkts', G, xa, precision=EXACT_DOT)  8.42 us
    dot_general x2, matrix products, block_grads(): jnp.einsum('gkts,tgkp->sgkp', mixing, G, precision=EXACT_DOT)  6.38 us
    rev x4, local copies, waits for them, and re-layouts, block_grads(): d_log = jnp.flip(jnp.cumsum(jnp.flip(d_cum, -1), axis=-1), -1)  5.96 us
    reduce_sum x1, other arithmetic, block_grads(): jnp.sum(lam * S0, axis=(-2, -1))  5.82 us
    split x6, local copies, waits for them, and re-layouts, causal_conv(): padded = jnp.concatenate([context, values], axis=0)  5.5 us
  transfers between devices with their start and end apart: 9, of which 1 were waited for; matrix products, arithmetic and copies ran while one was open for 60% of the time, Pallas kernels for 0%

profile of v1, /device:TPU:1, one launch (start us, length us, event | category | flops | bytes accessed | tf_op | source)
XLA Modules:
  0.0 231.6 jit_solution(3632879325709645542)
XLA Ops:
  7.2 1.5 compare_select_fusion.7
  11.4 2.7 %collective-permute-start = (f32[7712]{0:T(1024)S(1)}, f32[7712]{0:T(1024)S(1)}, u32[]{:S(2)}, u32[]{:S(2)}) collective-permute-start(f32[7712]{0:T(1024)S(1)} %pad_maximum_fusion.10), channel_id=1, source_target_pairs={{0,4},{4,8},{8,12},{12,0},{1,5},{5,9},{9,13},{13,1},{2,6},{6,10},{... | collective-permute-start | bytes 92552 | tf_op jit(solution)/shard_map/ppermute | solution.py:210
  16.0 1.4 exponential_multiply_fusion.1
  20.6 1.3 copy.232
  23.3 1.5 slice_convert_fusion.6
  31.5 2.7 %fusion.69 = f32[2,16,64,128]{3,2,1,0:T(8,128)} fusion(f32[128,2,16,64]{0,3,2,1:T(8,128)S(1)} %bitcast.285, f32[128,2,16]{0,2,1:T(8,128)} %exponential_bitcast_fusion.2, f32[128,2,128,1]{2,1,0,3:T(2,128)S(1)} %bitcast.300), kind=kOutput, calls=%fused_computation.110 | convolution fusion | flops 402915328 | bytes 2244608 | tf_op jit(solution)/shard_map/vmap(gkt,tgkp,tgn->gkpn)/dot_general | solution.py:270
  34.4 2.0 fusion.72
  37.5 1.5 copy.229
  39.1 1.8 convolution_bitcast_fusion.3
  41.9 1.4 pad_maximum_fusion
  44.7 1.3 copy.247
  51.5 1.3 exponential_bitcast_fusion
  52.9 1.4 compare_select_fusion.5
  54.4 1.4 slice.378
  57.1 2.1 copy.293
  60.5 1.3 mul.887
  61.9 1.3 mul.889
  66.6 3.3 %fusion.22 = f32[1,128,2,16,64]{1,4,3,2,0:T(8,128)S(1)} fusion(f32[128,2,16,64]{0,3,2,1:T(8,128)S(1)} %bitcast.286, f32[1,128,2,16,64]{1,4,3,2,0:T(8,128)S(1)} %bitcast.287, f32[2,16,128]{2,1,0:T(8,128)} %compare_select_fusion.5, f32[2,16,128]{2,1,0:T(8,128)} %bitcast.332, f32[2,128,128]{2,1,0:T(8,128)S(1)} %fusion.172, ...), kind=kOutput, calls=%fused_computation.42 | convolution fusion | flops 405798912 | bytes 3326080 | tf_op jit(solution)/shard_map/vmap(gkts,tgkp->sgkp)/dot_general | solution.py:120
  71.5 3.8 %broadcast_multiply_fusion = (f32[1,128,2048]{1,2,0:T(8,128)}, f32[1,128,2048]{1,2,0:T(8,128)}, f32[1,128,2048]{1,2,0:T(8,128)S(1)}) fusion(f32[2048]{0:T(1024)S(1)} %bitcast.336, f32[1,128,2,16,64]{1,4,3,2,0:T(8,128)S(1)} %fusion.22, f32[1,128,2048]{1,2,0:T(8,128)S(1)} %copy-done.7, f32[2048]{0:T(1024)S(1)} %bitcast.324, f32[1,3,2048]{1,2,0:T(8,128)S(1)} %bitcast.297, ...), kind=kLoop, calls=%fused_computation.125 | loop fusion | flops 5242880 | bytes 5300224 | tf_op jit(solution)/shard_map/vmap(transpose(jvp()))/mul | solution.py:49
  76.1 7.3 %multiply_reduce_fusion.2 = (f32[2,16,128]{2,1,0:T(8,128)}, f32[2,16,128]{2,1,0:T(8,128)}, f32[2,16,128]{2,1,0:T(8,128)}, f32[2,128,128]{2,1,0:T(8,128)}, f32[2,...) fusion(f32[2,16,128]{2,1,0:T(8,128)S(1)} %copy-done.82, ...), kind=kOutput, calls=%fused_computation.22 | convolution fusion | flops 415145984 | bytes 4898816 | tf_op jit(solution)/shard_map/vmap(tgkp,sgkp->gkts)/dot_general | solution.py:119
  84.2 2.4 %broadcast_multiply_fusion.1 = (f32[1,128,2048]{1,2,0:T(8,128)S(1)}, f32[1,128,2048]{1,2,0:T(8,128)S(1)}, f32[1,128,2048]{1,2,0:T(8,128)S(1)}) fusion(f32[1,128,2048]{1,2,0:T(8,128)} %get-tuple-element.118, f32[2048]{0:T(1024)S(1)} %bitcast.325, f32[2048]{0:T(1024)S(1)} %bitcast.321, f32[2048]{0:T(1024)S(1)} %bitcast.317), kind=kLoop, calls=%fused_computation.126 | loop fusion | flops 786432 | bytes 4218880 | tf_op jit(solution)/shard_map/vmap(transpose(jvp()))/mul | solution.py:49
  86.6 1.7 pad_add_fusion
  89.5 2.1 copy.254
  91.7 1.9 fusion.173
  93.6 1.7 copy.249
  98.7 1.4 convolution_bitcast_fusion.5
  100.7 31.9 %all-gather.3.cloned.1.call-done = f32[8,2,16,64,128]{4,3,2,1,0:T(8,128)} async-done(((f32[2,2,16,64,128]{4,3,2,1,0:T(8,128)}), f32[8,2,16,64,128]{4,3,2,1,0:T(8,128)}) %all-gather.3.cloned.1.call-update) | async-done | bytes 8388624 | tf_op jit(solution)/shard_map/all_gather | solution.py:244
  132.6 5.8 %multiply_reduce_fusion.5 = (f32[2,16]{1,0:T(2,128)}, f32[2,16,64,128]{3,2,1,0:T(8,128)S(1)}, f32[2,16,64,128]{3,2,1,0:T(8,128)}, f32[2,16,64,128]{3,2,1,0:T(8,128)S(1)}) fusion(pred[]{:T(512)S(6)} %eq.42, pred[]{:T(512)S(6)} %eq.43, f32[4,2,2,16,64,128]{5,4,3,2,1,0:T(8,128)} %bitcast.296, f32[2,16]{1,0:T(2,128)} %mul.934, f32[2,16]{1,0:T(2,128)} %mul.887, ...), kind=kLoop, calls=%fused_computation.99 | loop fusion | flops 5504992 | bytes 11534980 | tf_op jit(solution)/shard_map/reduce_sum | solution.py:143
  138.4 1.7 fusion.30
  140.1 2.6 %fusion.31 = f32[2,128,128]{2,1,0:T(8,128)} fusion(f32[2,16,64,128]{3,2,1,0:T(8,128)S(1)} %get-tuple-element.115, bf16[128,2,16,64]{0,3,2,1:T(8,128)(2,1)S(1)} %bitcast.294, f32[128,2,16]{0,2,1:T(8,128)S(1)} %copy-done.37), kind=kOutput, calls=%fused_computation.47 | convolution fusion | flops 403177472 | bytes 1720320 | tf_op jit(solution)/shard_map/tgkp,gkpn->tgn/dot_general | solution.py:128
  142.7 1.7 fusion.29
  144.3 1.9 fusion.33
  148.0 1.4 pad_maximum_fusion.9
  150.7 2.6 %collective-permute-start.5 = (f32[3,2560]{1,0:T(4,128)}, f32[3,2560]{1,0:T(4,128)}, u32[]{:S(2)}, u32[]{:S(2)}) collective-permute-start(f32[3,2560]{1,0:T(4,128)} %pad_maximum_fusion.9), channel_id=1, source_target_pairs={{4,12},{5,13},{6,14},{7,15},{20,28},{21,29},{22,30},{23,31}} | collective-permute-start | bytes 92168 | tf_op jit(solution)/shard_map/ppermute | solution.py:293
  158.8 2.6 %multiply_reduce_fusion.6 = (f32[128,2,16]{0,2,1:T(8,128)}, f32[128,2,16,64]{0,3,2,1:T(8,128)}) fusion(f32[128,2048]{0,1:T(8,128)S(1)} %copy.229, f32[2,16,64,128]{3,2,1,0:T(8,128)S(1)} %copy-done.4, f32[128,2,128,1]{2,1,0,3:T(2,128)S(1)} %bitcast.299), kind=kOutput, calls=%fused_computation.100 | convolution fusion | flops 403173376 | bytes 3293184 | tf_op jit(solution)/shard_map/gkpn,sgn->sgkp/dot_general | solution.py:137
  162.2 2.3 %fusion.139 = (f32[2,16]{1,0:T(2,128)}, f32[2,16,128]{1,0,2:T(2,128)S(1)}, f32[2,16,128]{1,0,2:T(2,128)}) fusion(f32[128,2,16]{2,1,0:T(2,128)S(1)} %copy.255, f32[2,16,128]{1,0,2:T(2,128)} %copy.226, f32[2,16,128]{1,0,2:T(2,128)S(1)} %copy-done.18), kind=kLoop, calls=%fused_computation.261 | loop fusion | flops 16352 | bytes 82048 | tf_op jit(solution)/shard_map/reduce_sum | solution.py:143
  165.3 3.1 %fusion.25 = f32[128,2,16,64]{0,3,2,1:T(8,128)S(1)} fusion(bf16[128,2,16,64]{0,3,2,1:T(8,128)(2,1)S(1)} %bitcast.295, f32[128,2,16,64]{0,3,2,1:T(8,128)} %get-tuple-element.185, f32[2,16,128]{2,1,0:T(8,128)} %bitcast.340, f32[2,16,128]{2,1,0:T(8,128)} %copy-done.41, f32[2,128,128]{2,1,0:T(8,128)} %copy-done.48, pred[128,128]{1,0:T(8,128)(4,1)} %iota_compare_fusion, ...), kind=kOutput, calls=%fused_computation.43 | convolution fusion | flops 406585344 | bytes 2818176 | tf_op jit(solution)/shard_map/gkts,tgkp->sgkp/dot_general | solution.py:120
  169.7 1.7 broadcast_multiply_fusion.4
  174.9 1.4 rev.16
  176.3 1.9 reduce_window_sum.53
  178.1 1.4 rev.17
  180.3 1.4 exponential_multiply_fusion
  181.8 1.5 copy.259
  183.3 1.7 bitcast_add_fusion
  184.9 1.6 copy.261
  186.5 1.3 sub.139
  187.9 1.5 copy.262
  189.3 1.7 fusion.140
  191.0 1.3 fusion.148
  192.4 1.6 rev.14
  194.0 1.6 copy.263
  195.5 1.9 reduce_window_sum.52
  197.4 1.5 copy.264
  198.9 1.6 copy.257
  200.4 1.3 add.385
  201.8 1.5 copy.265
  203.2 1.7 multiply_subtract_fusion
  204.9 1.6 copy.266
  206.5 1.5 fusion.145
  208.0 3.1 %convolution_bitcast_fusion.8 = f32[128,2,128]{0,2,1:T(8,128)S(1)} fusion(f32[2,16,64,128]{3,2,1,0:T(8,128)} %get-tuple-element.116, f32[2,16,128,64]{2,3,1,0:T(8,128)S(1)} %bitcast.284, f32[2,16,128]{2,1,0:T(8,128)} %copy.238), kind=kOutput, calls=%fused_computation.53 | convolution fusion | flops 402915328 | bytes 2244608 | tf_op jit(solution)/shard_map/gkpn,sgkp,gks->sgn/dot_general | solution.py:139
  212.7 2.4 %collective-permute-start.3 = (f32[3,2560]{1,0:T(4,128)S(1)}, f32[3,2560]{1,0:T(4,128)S(1)}, u32[]{:S(2)}, u32[]{:S(2)}) collective-permute-start(f32[3,2560]{1,0:T(4,128)S(1)} %pad_maximum_fusion.8), channel_id=1, source_target_pairs={{4,0},{8,4},{12,8},{5,1},{9,5},{13,9},{6,2},{10,6},{14,10},{7,3},{... | collective-permute-start | bytes 92168 | tf_op jit(solution)/shard_map/ppermute | solution.py:18
  215.1 1.6 split.67
  216.7 1.5 split.56
  223.4 1.4 scatter-add.14
  (306 shorter events, 59.7 us)
Async XLA Ops:
  7.2 19.1 %copy-start.25 = (bf16[128,2048]{1,0:T(8,128)(2,1)S(1)}, bf16[128,2048]{1,0:T(8,128)(2,1)}, u32[]{:S(2)}) copy-start(bf16[128,2048]{1,0:T(8,128)(2,1)} %param.27) | copy-start | bytes 1572868
  7.2 19.1 %copy-start.50 = (bf16[128,256]{1,0:T(8,128)(2,1)S(1)}, bf16[128,256]{1,0:T(8,128)(2,1)}, u32[]{:S(2)}) copy-start(bf16[128,256]{1,0:T(8,128)(2,1)} %param.28) | copy-start | bytes 196612
  7.2 19.0 %copy-start.49 = (bf16[128,256]{1,0:T(8,128)(2,1)S(1)}, bf16[128,256]{1,0:T(8,128)(2,1)}, u32[]{:S(2)}) copy-start(bf16[128,256]{1,0:T(8,128)(2,1)} %param.29) | copy-start | bytes 196612
  7.2 93.5 %all-reduce.26.cloned.1.call-start = ((), (), s32[]{:S(2)}) async-start(), calls=%async_computation | async-start | bytes 2097152 | tf_op jit(solution)/shard_map/psum | solution.py:286
  11.4 17.3 %collective-permute-start = (f32[7712]{0:T(1024)S(1)}, f32[7712]{0:T(1024)S(1)}, u32[]{:S(2)}, u32[]{:S(2)}) collective-permute-start(f32[7712]{0:T(1024)S(1)} %pad_maximum_fusion.10), channel_id=1, source_target_pairs={{0,4},{4,8},{8,12},{12,0},{1,5},{5,9},{9,13},{13,1},{2,6},{6,10},{... | collective-permute-start | bytes 92552 | tf_op jit(solution)/shard_map/ppermute | solution.py:210
  14.1 14.7 %collective-permute-start.1 = (f32[7712]{0:T(1024)S(1)}, f32[7712]{0:T(1024)S(1)}, u32[]{:S(2)}, u32[]{:S(2)}) collective-permute-start(f32[7712]{0:T(1024)S(1)} %pad_maximum_fusion.10), channel_id=1, source_target_pairs={{0,8},{4,12},{8,0},{12,4},{1,9},{5,13},{9,1},{13,5},{2,10},{6,14},... | collective-permute-start | bytes 92552 | tf_op jit(solution)/shard_map/ppermute | solution.py:210
  14.1 14.8 %collective-permute-start.2 = (f32[7712]{0:T(1024)S(1)}, f32[7712]{0:T(1024)S(1)}, u32[]{:S(2)}, u32[]{:S(2)}) collective-permute-start(f32[7712]{0:T(1024)S(1)} %pad_maximum_fusion.10), channel_id=1, source_target_pairs={{0,12},{4,0},{8,4},{12,8},{1,13},{5,1},{9,5},{13,9},{2,14},{6,2},{... | collective-permute-start | bytes 92552 | tf_op jit(solution)/shard_map/ppermute | solution.py:210
  15.3 4.7 %copy-start.80 = (f32[2,16]{1,0:T(2,128)}, f32[2,16]{1,0:T(2,128)S(1)}, u32[]{:S(2)}) copy-start(f32[2,16]{1,0:T(2,128)S(1)} %mul.858) | copy-start | bytes 388
  16.0 4.0 %copy-start.86 = (f32[2,16]{1,0:T(2,128)}, f32[2,16]{1,0:T(2,128)S(1)}, u32[]{:S(2)}) copy-start(f32[2,16]{1,0:T(2,128)S(1)} %add.346) | copy-start | bytes 388
  18.3 12.2 %copy-start.71 = (f32[1,256]{1,0:T(1,128)}, f32[1,256]{1,0:T(1,128)S(1)}, u32[]{:S(2)}) copy-start(f32[1,256]{1,0:T(1,128)S(1)} %get-tuple-element.180) | copy-start | bytes 3076
  18.3 12.2 %copy-start.73 = (f32[1,256]{1,0:T(1,128)}, f32[1,256]{1,0:T(1,128)S(1)}, u32[]{:S(2)}) copy-start(f32[1,256]{1,0:T(1,128)S(1)} %get-tuple-element.181) | copy-start | bytes 3076
  18.3 12.2 %copy-start.75 = (f32[1,256]{1,0:T(1,128)}, f32[1,256]{1,0:T(1,128)S(1)}, u32[]{:S(2)}) copy-start(f32[1,256]{1,0:T(1,128)S(1)} %get-tuple-element.183) | copy-start | bytes 3076
  18.3 12.2 %copy-start.77 = (f32[1,256]{1,0:T(1,128)}, f32[1,256]{1,0:T(1,128)S(1)}, u32[]{:S(2)}) copy-start(f32[1,256]{1,0:T(1,128)S(1)} %get-tuple-element.182) | copy-start | bytes 3076
  19.2 11.4 %copy-start.59 = (f32[1,256]{1,0:T(1,128)}, f32[1,256]{1,0:T(1,128)S(1)}, u32[]{:S(2)}) copy-start(f32[1,256]{1,0:T(1,128)S(1)} %get-tuple-element.176) | copy-start | bytes 3076
  19.2 11.4 %copy-start.62 = (f32[1,256]{1,0:T(1,128)}, f32[1,256]{1,0:T(1,128)S(1)}, u32[]{:S(2)}) copy-start(f32[1,256]{1,0:T(1,128)S(1)} %get-tuple-element.177) | copy-start | bytes 3076
  19.2 11.4 %copy-start.65 = (f32[1,256]{1,0:T(1,128)}, f32[1,256]{1,0:T(1,128)S(1)}, u32[]{:S(2)}) copy-start(f32[1,256]{1,0:T(1,128)S(1)} %get-tuple-element.179) | copy-start | bytes 3076
  19.2 11.4 %copy-start.68 = (f32[1,256]{1,0:T(1,128)}, f32[1,256]{1,0:T(1,128)S(1)}, u32[]{:S(2)}) copy-start(f32[1,256]{1,0:T(1,128)S(1)} %get-tuple-element.178) | copy-start | bytes 3076
  20.6 6.8 %copy-start.43 = (f32[1,2,16,128]{3,2,1,0:T(8,128)}, f32[1,2,16,128]{3,2,1,0:T(8,128)S(1)}, u32[]{:S(2)}) copy-start(f32[1,2,16,128]{3,2,1,0:T(8,128)S(1)} %reduce_window_sum.50) | copy-start | bytes 49156
  22.0 5.4 %copy-start.53 = (bf16[1,128,256]{2,1,0:T(8,128)(2,1)S(1)}, bf16[1,128,256]{2,1,0:T(8,128)(2,1)}, u32[]{:S(2)}) copy-start(bf16[1,128,256]{2,1,0:T(8,128)(2,1)} %param.34) | copy-start | bytes 196612
  22.0 5.4 %copy-start.54 = (bf16[1,128,256]{2,1,0:T(8,128)(2,1)S(1)}, bf16[1,128,256]{2,1,0:T(8,128)(2,1)}, u32[]{:S(2)}) copy-start(bf16[1,128,256]{2,1,0:T(8,128)(2,1)} %param.33) | copy-start | bytes 196612
  24.8 9.6 %copy-start.32 = (f32[1,2048]{1,0:T(1,128)}, f32[1,2048]{1,0:T(1,128)S(1)}, u32[]{:S(2)}) copy-start(f32[1,2048]{1,0:T(1,128)S(1)} %get-tuple-element.175) | copy-start | bytes 24580
  30.5 3.8 %copy-start.36 = (f32[3,2560]{1,0:T(4,128)}, f32[3,2560]{1,0:T(4,128)S(1)}, u32[]{:S(2)}) copy-start(f32[3,2560]{1,0:T(4,128)S(1)} %squeeze.24) | copy-start | bytes 92164
  30.6 3.8 %copy-start.5 = (f32[128,2048]{1,0:T(8,128)S(1)}, f32[128,2048]{1,0:T(8,128)}, u32[]{:S(2)}) copy-start(f32[128,2048]{1,0:T(8,128)} %convert_element_type.145) | copy-start | bytes 3145732
  30.6 3.8 %copy-start.45 = (f32[1,2048]{1,0:T(1,128)S(1)}, f32[1,2048]{1,0:T(1,128)}, u32[]{:S(2)}) copy-start(f32[1,2048]{1,0:T(1,128)} %get-tuple-element.174) | copy-start | bytes 24580
  34.4 98.3 %all-gather.3.cloned.1.call-start = ((), (), s32[]{:S(2)}) async-start(), calls=%async_computation.1 | async-start | bytes 10485760 | tf_op jit(solution)/shard_map/all_gather | solution.py:244
  47.9 8.2 %copy-start.17 = (f32[2,16,128]{1,0,2:T(2,128)}, f32[2,16,128]{1,0,2:T(2,128)S(1)}, u32[]{:S(2)}) copy-start(f32[2,16,128]{1,0,2:T(2,128)S(1)} %copy.221) | copy-start | bytes 49156
  54.4 15.5 %copy-start.16 = (f32[128,2,128]{0,2,1:T(8,128)}, f32[128,2,128]{0,2,1:T(8,128)S(1)}, u32[]{:S(2)}) copy-start(f32[128,2,128]{0,2,1:T(8,128)S(1)} %copy.248) | copy-start | bytes 393220
  55.9 14.0 %copy-start.19 = (f32[128,2,128]{0,2,1:T(8,128)}, f32[128,2,128]{0,2,1:T(8,128)S(1)}, u32[]{:S(2)}) copy-start(f32[128,2,128]{0,2,1:T(8,128)S(1)} %copy.237) | copy-start | bytes 393220
  56.0 13.9 %copy-start.21 = (f32[128,2,128]{0,2,1:T(8,128)}, f32[128,2,128]{0,2,1:T(8,128)S(1)}, u32[]{:S(2)}) copy-start(f32[128,2,128]{0,2,1:T(8,128)S(1)} %copy.241) | copy-start | bytes 393220
  57.1 12.8 %copy-start.15 = (f32[1,128,256]{1,2,0:T(8,128)}, f32[1,128,256]{1,2,0:T(8,128)S(1)}, u32[]{:S(2)}) copy-start(f32[1,128,256]{1,2,0:T(8,128)S(1)} %copy.296) | copy-start | bytes 393220
  66.6 9.1 %copy-start.48 = (f32[2,128,128]{2,1,0:T(8,128)}, f32[2,128,128]{2,1,0:T(8,128)S(1)}, u32[]{:S(2)}) copy-start(f32[2,128,128]{2,1,0:T(8,128)S(1)} %fusion.170) | copy-start | bytes 393220
  76.1 8.1 %copy-start.34 = (f32[1,2048]{1,0:T(1,128)S(1)}, f32[1,2048]{1,0:T(1,128)}, u32[]{:S(2)}) copy-start(f32[1,2048]{1,0:T(1,128)} %copy-done.32) | copy-start | bytes 24580
  132.6 5.8 %copy-start.37 = (f32[128,2,16]{0,2,1:T(8,128)S(1)}, f32[128,2,16]{0,2,1:T(8,128)}, u32[]{:S(2)}) copy-start(f32[128,2,16]{0,2,1:T(8,128)} %get-tuple-element.168) | copy-start | bytes 49156
  138.4 4.2 %copy-start.38 = (f32[128,2,16]{0,2,1:T(8,128)S(1)}, f32[128,2,16]{0,2,1:T(8,128)}, u32[]{:S(2)}) copy-start(f32[128,2,16]{0,2,1:T(8,128)} %exponential_bitcast_fusion) | copy-start | bytes 49156
  142.7 3.7 %copy-start.27 = (f32[1,128,256]{2,1,0:T(8,128)S(1)}, f32[1,128,256]{2,1,0:T(8,128)}, u32[]{:S(2)}) copy-start(f32[1,128,256]{2,1,0:T(8,128)} %get-tuple-element.189) | copy-start | bytes 393220
  144.3 10.2 %copy-start.22 = (f32[128,2,128]{0,2,1:T(8,128)S(1)}, f32[128,2,128]{0,2,1:T(8,128)}, u32[]{:S(2)}) copy-start(f32[128,2,128]{0,2,1:T(8,128)} %copy-done.21) | copy-start | bytes 393220
  144.3 10.2 %copy-start.28 = (f32[2,128,128]{2,1,0:T(8,128)S(1)}, f32[2,128,128]{2,1,0:T(8,128)}, u32[]{:S(2)}) copy-start(f32[2,128,128]{2,1,0:T(8,128)} %get-tuple-element.104) | copy-start | bytes 393220
  144.3 11.6 %copy-start.26 = (f32[128,256]{1,0:T(8,128)S(1)}, f32[128,256]{1,0:T(8,128)}, u32[]{:S(2)}) copy-start(f32[128,256]{1,0:T(8,128)} %get-tuple-element.187) | copy-start | bytes 393220
  147.1 11.7 %copy-start.4 = (f32[2,16,64,128]{3,2,1,0:T(8,128)S(1)}, f32[2,16,64,128]{3,2,1,0:T(8,128)}, u32[]{:S(2)}) copy-start(f32[2,16,64,128]{3,2,1,0:T(8,128)} %get-tuple-element.116) | copy-start | bytes 3145732
  147.9 7.9 %copy-start.30 = (f32[1,131,256]{2,1,0:T(8,128)}, f32[1,131,256]{2,1,0:T(8,128)S(1)}, u32[]{:S(2)}) copy-start(f32[1,131,256]{2,1,0:T(8,128)S(1)} %pad_add_fusion.2) | copy-start | bytes 402436
  148.0 8.7 %copy-start.57 = (f32[3,256]{1,0:T(4,128)}, f32[3,256]{1,0:T(4,128)S(1)}, u32[]{:S(2)}) copy-start(f32[3,256]{1,0:T(4,128)S(1)} %slice_bitcast_fusion.8) | copy-start | bytes 9220
  149.4 70.4 %collective-permute-start.4 = (f32[3,2560]{1,0:T(4,128)}, f32[3,2560]{1,0:T(4,128)}, u32[]{:S(2)}, u32[]{:S(2)}) collective-permute-start(f32[3,2560]{1,0:T(4,128)} %pad_maximum_fusion.9), channel_id=1, source_target_pairs={{0,12},{1,13},{2,14},{3,15},{16,28},{17,29},{18,30},{19,31}} | collective-permute-start | bytes 92168 | tf_op jit(solution)/shard_map/ppermute | solution.py:293
  150.7 69.1 %collective-permute-start.5 = (f32[3,2560]{1,0:T(4,128)}, f32[3,2560]{1,0:T(4,128)}, u32[]{:S(2)}, u32[]{:S(2)}) collective-permute-start(f32[3,2560]{1,0:T(4,128)} %pad_maximum_fusion.9), channel_id=1, source_target_pairs={{4,12},{5,13},{6,14},{7,15},{20,28},{21,29},{22,30},{23,31}} | collective-permute-start | bytes 92168 | tf_op jit(solution)/shard_map/ppermute | solution.py:293
  153.3 66.5 %collective-permute-start.6 = (f32[3,2560]{1,0:T(4,128)}, f32[3,2560]{1,0:T(4,128)}, u32[]{:S(2)}, u32[]{:S(2)}) collective-permute-start(f32[3,2560]{1,0:T(4,128)} %pad_maximum_fusion.9), channel_id=1, source_target_pairs={{8,12},{9,13},{10,14},{11,15},{24,28},{25,29},{26,30},{27,31}} | collective-permute-start | bytes 92168 | tf_op jit(solution)/shard_map/ppermute | solution.py:293
  157.4 3.9 %copy-start.11 = (f32[128,256]{1,0:T(8,128)}, f32[128,256]{1,0:T(8,128)S(1)}, u32[]{:S(2)}) copy-start(f32[128,256]{1,0:T(8,128)S(1)} %get-tuple-element.158) | copy-start | bytes 393220
  157.5 3.9 %copy-start.13 = (f32[128,256]{1,0:T(8,128)}, f32[128,256]{1,0:T(8,128)S(1)}, u32[]{:S(2)}) copy-start(f32[128,256]{1,0:T(8,128)S(1)} %get-tuple-element.159) | copy-start | bytes 393220
  158.2 4.0 %copy-start.18 = (f32[2,16,128]{1,0,2:T(2,128)S(1)}, f32[2,16,128]{1,0,2:T(2,128)}, u32[]{:S(2)}) copy-start(f32[2,16,128]{1,0,2:T(2,128)} %copy-done.17) | copy-start | bytes 49156
  173.0 7.3 %copy-start.39 = (f32[32,1,128]{2,1,0:T(1,128)S(1)}, f32[32,1,128]{2,1,0:T(1,128)}, u32[]{:S(2)}) copy-start(f32[32,1,128]{2,1,0:T(1,128)} %param.35) | copy-start | bytes 49156
  181.8 24.7 %copy-start.40 = (f32[32,128]{1,0:T(8,128)S(1)}, f32[32,128]{1,0:T(8,128)}, u32[]{:S(2)}) copy-start(f32[32,128]{1,0:T(8,128)} %param.30) | copy-start | bytes 49156
  191.0 20.0 %copy-start.20 = (f32[128,2,128]{0,2,1:T(8,128)S(1)}, f32[128,2,128]{0,2,1:T(8,128)}, u32[]{:S(2)}) copy-start(f32[128,2,128]{0,2,1:T(8,128)} %copy-done.19) | copy-start | bytes 393220
  206.5 4.6 %copy-start.29 = (f32[2,128,128]{2,1,0:T(8,128)S(1)}, f32[2,128,128]{2,1,0:T(8,128)}, u32[]{:S(2)}) copy-start(f32[2,128,128]{2,1,0:T(8,128)} %get-tuple-element.104) | copy-start | bytes 393220
  208.0 3.6 %copy-start.70 = (f32[1,256]{1,0:T(1,128)S(1)}, f32[1,256]{1,0:T(1,128)}, u32[]{:S(2)}) copy-start(f32[1,256]{1,0:T(1,128)} %copy-done.68) | copy-start | bytes 3076
  208.0 4.5 %copy-start.61 = (f32[1,256]{1,0:T(1,128)S(1)}, f32[1,256]{1,0:T(1,128)}, u32[]{:S(2)}) copy-start(f32[1,256]{1,0:T(1,128)} %copy-done.59) | copy-start | bytes 3076
  208.0 4.6 %copy-start.64 = (f32[1,256]{1,0:T(1,128)S(1)}, f32[1,256]{1,0:T(1,128)}, u32[]{:S(2)}) copy-start(f32[1,256]{1,0:T(1,128)} %copy-done.62) | copy-start | bytes 3076
  208.0 4.6 %copy-start.67 = (f32[1,256]{1,0:T(1,128)S(1)}, f32[1,256]{1,0:T(1,128)}, u32[]{:S(2)}) copy-start(f32[1,256]{1,0:T(1,128)} %copy-done.65) | copy-start | bytes 3076
  211.1 7.8 %copy-start.10 = (bf16[131,2048]{1,0:T(8,128)(2,1)S(1)}, bf16[131,2048]{1,0:T(8,128)(2,1)}, u32[]{:S(2)}) copy-start(bf16[131,2048]{1,0:T(8,128)(2,1)} %pad_add_fusion.1) | copy-start | bytes 1609732
  211.4 8.4 %copy-start.31 = (f32[3,2048]{1,0:T(4,128)S(1)}, f32[3,2048]{1,0:T(4,128)}, u32[]{:S(2)}) copy-start(f32[3,2048]{1,0:T(4,128)} %copy.254) | copy-start | bytes 73732
  211.4 8.4 %copy-start.56 = (f32[3,256]{1,0:T(4,128)S(1)}, f32[3,256]{1,0:T(4,128)}, u32[]{:S(2)}) copy-start(f32[3,256]{1,0:T(4,128)} %slice_bitcast_fusion.9) | copy-start | bytes 9220
  211.4 8.4 %copy-start.58 = (f32[3,256]{1,0:T(4,128)S(1)}, f32[3,256]{1,0:T(4,128)}, u32[]{:S(2)}) copy-start(f32[3,256]{1,0:T(4,128)} %copy-done.57) | copy-start | bytes 9220
  211.4 9.3 %copy-start.12 = (f32[128,256]{1,0:T(8,128)S(1)}, f32[128,256]{1,0:T(8,128)}, u32[]{:S(2)}) copy-start(f32[128,256]{1,0:T(8,128)} %copy-done.11) | copy-start | bytes 393220
  211.4 9.3 %copy-start.14 = (f32[128,256]{1,0:T(8,128)S(1)}, f32[128,256]{1,0:T(8,128)}, u32[]{:S(2)}) copy-start(f32[128,256]{1,0:T(8,128)} %copy-done.13) | copy-start | bytes 393220
  212.6 8.1 %copy-start.1 = (f32[128,2048]{1,0:T(8,128)S(1)}, f32[128,2048]{1,0:T(8,128)}, u32[]{:S(2)}) copy-start(f32[128,2048]{1,0:T(8,128)} %copy-done) | copy-start | bytes 3145732
  212.6 8.1 %copy-start.3 = (f32[128,2048]{1,0:T(8,128)S(1)}, f32[128,2048]{1,0:T(8,128)}, u32[]{:S(2)}) copy-start(f32[128,2048]{1,0:T(8,128)} %copy-done.2) | copy-start | bytes 3145732
  212.7 7.1 %collective-permute-start.3 = (f32[3,2560]{1,0:T(4,128)S(1)}, f32[3,2560]{1,0:T(4,128)S(1)}, u32[]{:S(2)}, u32[]{:S(2)}) collective-permute-start(f32[3,2560]{1,0:T(4,128)S(1)} %pad_maximum_fusion.8), channel_id=1, source_target_pairs={{4,0},{8,4},{12,8},{5,1},{9,5},{13,9},{6,2},{10,6},{14,10},{7,3},{... | collective-permute-start | bytes 92168 | tf_op jit(solution)/shard_map/ppermute | solution.py:18
  (33 other events, 56.0 us)
Sparse Core Ops, SparseCore 0:
  34.5 36.9 all-reduce.25
  73.0 59.5 all-gather.2
